TPU v7x, 32 devices: a whole 2x2x4 slice. The times are simulated.
32 devices in a mesh: ckpt: 2 (over x), train: 4 (over z), tensor: 4 (over y, core).
Axes of the slice: x: 2, y: 2, z: 4, core: 2. Of those that a mesh axis runs over, the one named last changes fastest.
Arguments:
- hidden: bfloat16 [2, 2048, 28672], P('ckpt', 'train', 'tensor'), may hold values from -6 to 6
- out_grads: bfloat16 [2, 2048, 8192], P('ckpt', 'train', 'tensor'), may hold values from -6 to 6
- proj_in: bfloat16 [64, 28672], P(None, 'tensor'), may hold values from -0.03125 to 0.03125
- proj_out: bfloat16 [64, 8192], P(None, 'tensor'), may hold values from -0.0625 to 0.0625
- test_grads: bfloat16 [2, 64, 4096], P('ckpt', ('train', 'tensor')), may hold values from -6 to 6
- step_weights: int32 [2], P('ckpt'), may hold values from 1 to 4
Outputs:
- scores: float32 [16, 4, 16], P('train', None, 'tensor')
All inputs are finite; a program needn't handle non-finite values.
Results may differ from a plain program's by a relative error of at most 0.0029.
Values may be sent and summed in bfloat16 or wider, within the bound.
No kernel may reach another device: no remote copies, remote signals or barrier semaphores. Data moves between devices by JAX's collectives and lax.ppermute only.
A program may use at most 64 MiB of HBM per device.

v0:
```python
import math
import jax
import jax.numpy as jnp
from jax import lax
from jax.sharding import PartitionSpec as P

KIN = 64
KOUT = 64
SEQ = 128


def outer_grads(sides):
    blocks = sides.reshape(-1, SEQ, KIN + KOUT)
    left = blocks[:, :, :KIN]
    right = blocks[:, :, KIN:]
    outer = jnp.einsum("sto,sti->soi", right, left, precision=lax.Precision.HIGHEST)
    return outer.reshape(-1, KIN * KOUT).astype(jnp.bfloat16)


def body(hidden, out_grads, proj_in, proj_out, test_grads, step_weights):
    train_count = lax.axis_size("train")
    h_local = hidden[0]
    g_local = out_grads[0]
    contract = (((1,), (1,)), ((), ()))
    left = lax.dot_general(h_local, proj_in, contract, preferred_element_type=jnp.float32)
    right = lax.dot_general(g_local, proj_out, contract, preferred_element_type=jnp.float32)
    shared = lax.psum_scatter(
        jnp.concatenate([left, right], axis=1), "tensor", scatter_dimension=0, tiled=True
    )
    own = outer_grads(shared)
    train_block = lax.all_gather(own, "tensor", axis=0, tiled=True)
    tests = test_grads[0]
    width = tests.shape[0]
    examples = train_block.shape[0]
    table = lax.dot_general(
        train_block,
        lax.all_gather(test_grads, "train", axis=1, tiled=True)[0],
        contract,
        preferred_element_type=jnp.float32,
    )
    scale = 1.0 / math.sqrt(SEQ * KIN * KOUT)
    weight = step_weights[0].astype(jnp.float32) * scale
    total = lax.psum(table * weight, "ckpt")
    return total.reshape(examples, train_count, width)


def solution(mesh):
    placed = (
        P("ckpt", "train", "tensor"),
        P("ckpt", "train", "tensor"),
        P(None, "tensor"),
        P(None, "tensor"),
        P("ckpt", ("train", "tensor"), None),
        P("ckpt"),
    )
    return jax.shard_map(
        body, mesh=mesh, in_specs=placed, out_specs=P("train", None, "tensor"), check_vma=False
    )
```

profile of v0, /device:TPU:0, one launch (start us, length us, event | category | flops | bytes accessed | tf_op | source)
XLA Modules:
  0.0 55.8 jit_solution(17442658351243271955)
XLA Ops:
  6.5 0.0 copy-start
  6.5 0.0 copy-start.1
  6.5 0.0 copy-start.2
  6.5 0.0 reduce-scatter.2.cloned.1.call-start
  6.5 5.8 %fusion = f32[512,64]{0,1:T(8,128)S(1)} fusion(bf16[64,7168]{1,0:T(8,128)(2,1)} %param.8, bf16[1,512,7168]{2,1,0:T(8,128)(2,1)} %param.6), kind=kOutput, calls=%fused_computation | convolution fusion | flops 469762048 | bytes 8388608 | tf_op jit(solution)/shard_map/dot_general | solution.py:25
  12.3 0.0 copy-done
  12.3 0.0 copy-done.1
  12.3 0.8 %fusion.2 = f32[512,64]{0,1:T(8,128)S(1)} fusion(bf16[64,2048]{1,0:T(8,128)(2,1)S(1)} %copy-done.1, bf16[1,512,2048]{2,1,0:T(8,128)(2,1)S(1)} %copy-done), kind=kOutput, calls=%fused_computation.2 | convolution fusion | flops 134217728 | bytes 2490368 | tf_op jit(solution)/shard_map/dot_general | solution.py:26
  13.1 0.7 %pad_maximum_fusion = f32[512,128]{0,1:T(8,128)} fusion(f32[512,64]{0,1:T(8,128)S(1)} %fusion.2, f32[512,64]{0,1:T(8,128)S(1)} %fusion), kind=kLoop, calls=%fused_computation.6 | loop fusion | flops 65536 | bytes 524288 | tf_op jit(solution)/shard_map/concatenate | solution.py:28
  13.8 0.0 reduce-scatter.2.cloned.1.call-update
  13.8 0.0 copy-done.2
  13.8 0.1 copy.9
  14.5 15.6 %all_gather.7 = bf16[1,16,4096]{2,0,1:T(2,128)(2,1)S(1)} all-gather(bf16[1,4,4096]{2,0,1:T(2,128)(2,1)S(1)} %copy.9), channel_id=1, replica_groups=mesh['ckpt'=2,'train'=4,'tensor'=4] {'train'}, dimensions={1}, use_global_device_ids=true | all-gather | bytes 163840 | tf_op jit(solution)/shard_map/all_gather | solution.py:37
  30.2 6.5 %reduce-scatter.2.cloned.1.call-done = f32[128,128]{0,1:T(8,128)} async-done(((f32[512,128]{0,1:T(8,128)}), f32[128,128]{0,1:T(8,128)}) %reduce-scatter.2.cloned.1.call-update) | async-done | bytes 65552 | tf_op jit(solution)/shard_map/reduce_scatter | solution.py:27
  36.7 1.0 %convolution_convert_fusion = bf16[64,64]{1,0:T(8,128)(2,1)S(1)} fusion(f32[1,128,128]{1,2,0:T(8,128)} %bitcast.22), kind=kOutput, calls=%fused_computation.4 | convolution fusion | flops 6295552 | bytes 73728 | tf_op jit(solution)/shard_map/sto,sti->soi/dot_general | solution.py:16
  37.7 0.1 reshape.35
  37.8 5.2 %all-gather = bf16[4,1,4096]{2,1,0:T(2,128)(2,1)S(1)} all-gather(bf16[1,1,4096]{2,1,0:T(2,128)(2,1)S(1)} %reshape.35), channel_id=1, replica_groups=mesh['ckpt'=2,'train'=4,'tensor'=4] {'tensor'}, dimensions={0}, use_global_device_ids=true | all-gather | bytes 40960 | tf_op jit(solution)/shard_map/all_gather | solution.py:31
  43.0 0.3 convolution_multiply_fusion
  43.3 0.1 reshape.34
  43.4 5.6 %psum.7 = f32[4,4,4]{2,1,0:T(4,128)} all-reduce(f32[4,4,4]{2,1,0:T(4,128)S(1)} %reshape.34), channel_id=1, replica_groups=mesh['ckpt'=2,'train'=4,'tensor'=4] {'ckpt'}, use_global_device_ids=true, to_apply=%region_1.0 | all-reduce | flops 64 | bytes 512 | tf_op jit(solution)/shard_map/psum | solution.py:43
Async XLA Ops:
  6.5 5.8 %copy-start = (bf16[1,512,2048]{2,1,0:T(8,128)(2,1)S(1)}, bf16[1,512,2048]{2,1,0:T(8,128)(2,1)}, u32[]{:S(2)}) copy-start(bf16[1,512,2048]{2,1,0:T(8,128)(2,1)} %param.7) | copy-start | bytes 6291460
  6.5 5.8 %copy-start.1 = (bf16[64,2048]{1,0:T(8,128)(2,1)S(1)}, bf16[64,2048]{1,0:T(8,128)(2,1)}, u32[]{:S(2)}) copy-start(bf16[64,2048]{1,0:T(8,128)(2,1)} %param.9) | copy-start | bytes 786436
  6.5 7.3 %copy-start.2 = (bf16[1,4,4096]{2,1,0:T(4,128)(2,1)S(1)}, bf16[1,4,4096]{2,1,0:T(4,128)(2,1)}, u32[]{:S(2)}) copy-start(bf16[1,4,4096]{2,1,0:T(4,128)(2,1)} %param.10) | copy-start | bytes 98308
  6.5 30.2 %reduce-scatter.2.cloned.1.call-start = ((), (), s32[]{:S(2)}) async-start(), calls=%async_computation.1 | async-start | bytes 327680 | tf_op jit(solution)/shard_map/reduce_scatter | solution.py:27
Sparse Core Ops, SparseCore 0:
  13.9 22.7 reduce-scatter.1
where the time goes:
time: 56 us; the launch traced here: 55.8 us
  blocking collectives  26.4 us (47%)
  between operations  14.1 us (25%)
  matrix products  7.76 us (14%)
  waiting for transfers between devices  6.55 us (12%)
  other arithmetic  0.72 us (1%)
    all_gather x1, blocking collectives, body(): lax.all_gather(test_grads, 'train', axis=1, tiled=True)[0]  15.6 us
    reduce_scatter x1, waiting for transfers between devices, body(): lax.psum_scatter(jnp.concatenate([left, right], axis=1), 'tensor', scatte...  6.54 us
    dot_general x1, matrix products, body(): lax.dot_general(h_local, proj_in, contract, preferred_element_type=jnp.fl...  5.76 us
    psum x1, blocking collectives, body(): total = lax.psum(table * weight, 'ckpt')  5.56 us
    all_gather x1, blocking collectives, body(): train_block = lax.all_gather(own, 'tensor', axis=0, tiled=True)  5.23 us
  transfers between devices with their start and end apart: 1, of which 1 were waited for; matrix products, arithmetic and copies ran while one was open for 0% of the time, Pallas kernels for 0%

commit v1 on v0

--- a/solution.py
+++ b/solution.py
@@ -7,6 +7,27 @@
 KIN = 64
 KOUT = 64
 SEQ = 128
+
+
+def _group_loads(frame_in):
+    prior, t_next, answer = (lax.axis_size("tensor"), lax.axis_index("tensor"), frame_in.shape[0])
+    heap = [(d, (d + 1) % prior) for d in range(prior)]
+    frames = [(d, (d - 1) % prior) for d in range(prior)]
+    wide_out = jnp.zeros((*frame_in.shape[:0], prior * answer, *frame_in.shape[1:]), frame_in.dtype)
+    wide_out = lax.dynamic_update_slice_in_dim(wide_out, frame_in, t_next * answer, axis=0)
+    near = mixed_arr = frame_in
+    ready = prior // 2
+    for src_i in tuple(range(1, ready + 1)):
+        near = lax.ppermute(near, "tensor", heap)
+        wide_out = lax.dynamic_update_slice_in_dim(
+            wide_out, near, (t_next - src_i) % prior * answer, axis=0
+        )
+        if src_i < prior - ready:
+            mixed_arr = lax.ppermute(mixed_arr, "tensor", frames)
+            wide_out = lax.dynamic_update_slice_in_dim(
+                wide_out, mixed_arr, (t_next + src_i) % prior * answer, axis=0
+            )
+    return wide_out
 
 
 def outer_grads(sides):
@@ -28,7 +49,7 @@
         jnp.concatenate([left, right], axis=1), "tensor", scatter_dimension=0, tiled=True
     )
     own = outer_grads(shared)
-    train_block = lax.all_gather(own, "tensor", axis=0, tiled=True)
+    train_block = _group_loads(own)
     tests = test_grads[0]
     width = tests.shape[0]
     examples = train_block.shape[0]

time: 56 us -> 69.5 us (1.24)
  waiting for transfers between devices: 6.55 us -> 24.2 us
  blocking collectives: 26.4 us -> 19.8 us
  starting transfers between devices: 0.01 us -> 1.78 us
    reduce_scatter x1, waiting for transfers between devices: 6.54 us -> 22.9 us  [body(): lax.psum_scatter(jnp.concatenate([left, right], axis=1), 'tensor', scatte...]
    all_gather x1 -> x0, blocking collectives: 5.23 us -> none  [body(): train_block = lax.all_gather(own, 'tensor', axis=0, tiled=True)]
    ppermute x0 -> x3, starting transfers between devices: none -> 1.78 us  [the longest x1 1.77 us: _group_loads(): mixed_arr = lax.ppermute(mixed_arr, 'tensor', frames)]
    all_gather x1, blocking collectives: 15.6 us -> 14.2 us  [body(): lax.all_gather(test_grads, 'train', axis=1, tiled=True)[0]]
    ppermute x0 -> x3, waiting for transfers between devices: none -> 1.31 us  [the longest x2 1.31 us: _group_loads(): near = lax.ppermute(near, 'tensor', heap)]
  transfers between devices with their start and end apart: 1 -> 4, of which waited for: 1 -> 2; matrix products, arithmetic and copies ran while one was open for 0% -> 1% of each run, Pallas kernels for 0% -> 0%
where the time goes in v1:
time: 69.5 us; the launch traced here: 69.3 us
  waiting for transfers between devices  24.2 us (35%)
  blocking collectives  19.8 us (28%)
  between operations  14.2 us (20%)
  matrix products  7.74 us (11%)
  starting transfers between devices  1.78 us (3%)
  local copies, waits for them, and re-layouts  0.88 us (1%)
  other arithmetic  0.71 us (1%)
    reduce_scatter x1, waiting for transfers between devices, body(): lax.psum_scatter(jnp.concatenate([left, right], axis=1), 'tensor', scatte...  22.9 us
    all_gather x1, blocking collectives, body(): lax.all_gather(test_grads, 'train', axis=1, tiled=True)[0]  14.2 us
    dot_general x1, matrix products, body(): lax.dot_general(h_local, proj_in, contract, preferred_element_type=jnp.fl...  5.76 us
    psum x1, blocking collectives, body(): total = lax.psum(table * weight, 'ckpt')  5.57 us
    ppermute x1, starting transfers between devices, _group_loads(): mixed_arr = lax.ppermute(mixed_arr, 'tensor', frames)  1.77 us
  transfers between devices with their start and end apart: 4, of which 2 were waited for; matrix products, arithmetic and copies ran while one was open for 1% of the time, Pallas kernels for 0%

profile of v1, /device:TPU:0, one launch (start us, length us, event | category | flops | bytes accessed | tf_op | source)
XLA Modules:
  0.0 69.3 jit_solution(11364030979759713573)
XLA Ops:
  6.5 0.0 copy-start
  6.5 0.0 copy-start.1
  6.5 0.0 copy-start.2
  6.5 0.0 reduce-scatter.2.cloned.1.call-start
  6.5 5.8 %fusion = f32[512,64]{0,1:T(8,128)S(1)} fusion(bf16[64,7168]{1,0:T(8,128)(2,1)} %param.8, bf16[1,512,7168]{2,1,0:T(8,128)(2,1)} %param.6), kind=kOutput, calls=%fused_computation | convolution fusion | flops 469762048 | bytes 8388608 | tf_op jit(solution)/shard_map/dot_general | solution.py:46
  12.3 0.0 copy-done
  12.3 0.0 copy-done.1
  12.3 0.8 %fusion.2 = f32[512,64]{0,1:T(8,128)S(1)} fusion(bf16[64,2048]{1,0:T(8,128)(2,1)S(1)} %copy-done.1, bf16[1,512,2048]{2,1,0:T(8,128)(2,1)S(1)} %copy-done), kind=kOutput, calls=%fused_computation.2 | convolution fusion | flops 134217728 | bytes 2490368 | tf_op jit(solution)/shard_map/dot_general | solution.py:47
  13.1 0.7 %pad_maximum_fusion = f32[512,128]{0,1:T(8,128)} fusion(f32[512,64]{0,1:T(8,128)S(1)} %fusion.2, f32[512,64]{0,1:T(8,128)S(1)} %fusion), kind=kLoop, calls=%fused_computation.6 | loop fusion | flops 65536 | bytes 524288 | tf_op jit(solution)/shard_map/concatenate | solution.py:49
  13.8 0.0 reduce-scatter.2.cloned.1.call-update
  13.8 22.9 %reduce-scatter.2.cloned.1.call-done = f32[128,128]{0,1:T(8,128)} async-done(((f32[512,128]{0,1:T(8,128)}), f32[128,128]{0,1:T(8,128)}) %reduce-scatter.2.cloned.1.call-update) | async-done | bytes 65552 | tf_op jit(solution)/shard_map/reduce_scatter | solution.py:48
  36.7 1.0 %convolution_convert_fusion = bf16[64,64]{1,0:T(8,128)(2,1)S(1)} fusion(f32[1,128,128]{1,2,0:T(8,128)} %bitcast.20), kind=kOutput, calls=%fused_computation.4 | convolution fusion | flops 6295552 | bytes 73728 | tf_op jit(solution)/shard_map/sto,sti->soi/dot_general | solution.py:37
  37.7 0.1 convert_element_type.19
  37.8 0.0 collective-permute-start
  37.8 0.0 copy-done.2
  37.8 0.1 copy.8
  37.8 1.8 %collective-permute-start.1 = (bf16[1,4096]{1,0:T(2,128)(2,1)S(1)}, bf16[1,4096]{1,0:T(2,128)(2,1)S(1)}, u32[]{:S(2)}, u32[]{:S(2)}) collective-permute-start(bf16[1,4096]{1,0:T(2,128)(2,1)S(1)} %convert_element_type.19), channel_id=1, source_target_pairs={{0,3},{1,0},{2,1},{3,2},{4,7},{5,4},{6,5},{7,6},{8,11},{9,8},{10,9... | collective-permute-start | bytes 24584 | tf_op jit(solution)/shard_map/ppermute | solution.py:26
  39.6 1.3 %collective-permute-done = bf16[1,4096]{1,0:T(2,128)(2,1)S(1)} collective-permute-done((bf16[1,4096]{1,0:T(2,128)(2,1)S(1)}, bf16[1,4096]{1,0:T(2,128)(2,1)S(1)}, u32[]{:S(2)}, u32[]{:S(2)}) %collective-permute-start) | collective-permute-done | bytes 8224 | tf_op jit(solution)/shard_map/ppermute | solution.py:21
  40.9 0.0 collective-permute-start.2
  40.9 14.2 %all_gather.3 = bf16[1,16,4096]{2,0,1:T(2,128)(2,1)S(1)} all-gather(bf16[1,4,4096]{2,0,1:T(2,128)(2,1)S(1)} %copy.8), channel_id=1, replica_groups=mesh['ckpt'=2,'train'=4,'tensor'=4] {'train'}, dimensions={1}, use_global_device_ids=true | all-gather | bytes 163840 | tf_op jit(solution)/shard_map/all_gather | solution.py:58
  55.8 0.2 dynamic_update_slice.12
  56.0 0.2 dynamic_update_slice.13
  56.2 0.0 collective-permute-done.1
  56.2 0.2 dynamic_update_slice.14
  56.4 0.0 collective-permute-done.2
  56.4 0.2 dynamic_update_slice.15
  56.5 0.3 convolution_multiply_fusion
  56.8 0.1 reshape.34
  56.9 5.6 %psum.7 = f32[4,4,4]{2,1,0:T(4,128)} all-reduce(f32[4,4,4]{2,1,0:T(4,128)S(1)} %reshape.34), channel_id=1, replica_groups=mesh['ckpt'=2,'train'=4,'tensor'=4] {'ckpt'}, use_global_device_ids=true, to_apply=%region_1.2 | all-reduce | flops 64 | bytes 512 | tf_op jit(solution)/shard_map/psum | solution.py:64
  (1 shorter events, 0.0 us)
Async XLA Ops:
  6.5 5.8 %copy-start = (bf16[1,512,2048]{2,1,0:T(8,128)(2,1)S(1)}, bf16[1,512,2048]{2,1,0:T(8,128)(2,1)}, u32[]{:S(2)}) copy-start(bf16[1,512,2048]{2,1,0:T(8,128)(2,1)} %param.7) | copy-start | bytes 6291460
  6.5 5.8 %copy-start.1 = (bf16[64,2048]{1,0:T(8,128)(2,1)S(1)}, bf16[64,2048]{1,0:T(8,128)(2,1)}, u32[]{:S(2)}) copy-start(bf16[64,2048]{1,0:T(8,128)(2,1)} %param.9) | copy-start | bytes 786436
  6.5 31.2 %copy-start.2 = (bf16[1,4,4096]{2,1,0:T(4,128)(2,1)S(1)}, bf16[1,4,4096]{2,1,0:T(4,128)(2,1)}, u32[]{:S(2)}) copy-start(bf16[1,4,4096]{2,1,0:T(4,128)(2,1)} %param.10) | copy-start | bytes 98308
  6.5 30.2 %reduce-scatter.2.cloned.1.call-start = ((), (), s32[]{:S(2)}) async-start(), calls=%async_computation.1 | async-start | bytes 327680 | tf_op jit(solution)/shard_map/reduce_scatter | solution.py:48
  37.8 3.2 %collective-permute-start = (bf16[1,4096]{1,0:T(2,128)(2,1)S(1)}, bf16[1,4096]{1,0:T(2,128)(2,1)S(1)}, u32[]{:S(2)}, u32[]{:S(2)}) collective-permute-start(bf16[1,4096]{1,0:T(2,128)(2,1)S(1)} %convert_element_type.19), channel_id=1, source_target_pairs={{0,1},{1,2},{2,3},{3,0},{4,5},{5,6},{6,7},{7,4},{8,9},{9,10},{10,1... | collective-permute-start | bytes 24584 | tf_op jit(solution)/shard_map/ppermute | solution.py:21
  37.8 18.3 %collective-permute-start.1 = (bf16[1,4096]{1,0:T(2,128)(2,1)S(1)}, bf16[1,4096]{1,0:T(2,128)(2,1)S(1)}, u32[]{:S(2)}, u32[]{:S(2)}) collective-permute-start(bf16[1,4096]{1,0:T(2,128)(2,1)S(1)} %convert_element_type.19), channel_id=1, source_target_pairs={{0,3},{1,0},{2,1},{3,2},{4,7},{5,4},{6,5},{7,6},{8,11},{9,8},{10,9... | collective-permute-start | bytes 24584 | tf_op jit(solution)/shard_map/ppermute | solution.py:26
  40.9 15.4 %collective-permute-start.2 = (bf16[1,4096]{1,0:T(2,128)(2,1)S(1)}, bf16[1,4096]{1,0:T(2,128)(2,1)S(1)}, u32[]{:S(2)}, u32[]{:S(2)}) collective-permute-start(bf16[1,4096]{1,0:T(2,128)(2,1)S(1)} %collective-permute-done), channel_id=1, source_target_pairs={{0,1},{1,2},{2,3},{3,0},{4,5},{5,6},{6,7},{7,4},{8,9},{9,10},{10,1... | collective-permute-start | bytes 24584 | tf_op jit(solution)/shard_map/ppermute | solution.py:21
Sparse Core Ops, SparseCore 0:
  13.9 22.7 reduce-scatter.1
